TPU v7x, 512 devices: a whole 4x8x8 slice. The times are simulated.
512 devices in a mesh: dp: 32 (over y, x), section: 4 (over z_hi), space: 4 (over z_lo, core).
Axes of the slice: x: 4, y: 8, z: 8 (z_hi: 4, z_lo: 2; z = z_hi * 2 + z_lo), core: 2. Of those that a mesh axis runs over, the one named last changes fastest.
Arguments:
- images: bfloat16 [64, 4, 64, 256], P('dp', 'space'), may hold values from -6 to 6
- steps: int32 [64], P('dp'), may hold values from 0 to 999
- out_grad: bfloat16 [64, 4, 64, 256], P('dp', 'space'), may hold values from -0.125 to 0.125
- conv_weight: bfloat16 [4, 3, 3, 256, 256], P('section'), may hold values from -0.125 to 0.125
- gn_gain: float32 [4, 256], P('section'), may hold values from 0.5 to 2
- emb_weight: bfloat16 [4, 256, 512], P('section'), may hold values from -0.375 to 0.375
Outputs:
- grad_conv: float32 [4, 3, 3, 256, 256], P('section')
- grad_gain: float32 [4, 256], P('section')
- grad_emb: float32 [4, 256, 512], P('section')
All inputs are finite; a program needn't handle non-finite values.
Results may differ from a plain program's by a relative error of at most 0.0064.
Values may be sent and summed in bfloat16 or wider, within the bound.
No kernel may reach another device: no remote copies, remote signals or barrier semaphores. Data moves between devices by JAX's collectives and lax.ppermute only.
A program may use at most 64 MiB of HBM per device.

v0:
```python
import math
import jax
import jax.numpy as jnp
from jax import lax
from jax.sharding import PartitionSpec as P

G = 32
FREQ = 256
MICRO = 2
EPS = 1e-05


def from_behind(value, axis, steps):
    count = lax.axis_size(axis)
    initial, last = (max(0, -steps), min(count, count - steps))
    return lax.ppermute(value, axis, [(source, source + steps) for source in range(initial, last)])


def extended(shard, sides, width):
    for axis, dim in sides:
        size, length = (lax.axis_size(axis), shard.shape[dim])
        up = [(i, (i + 1) % size) for i in range(size - 1)]
        down = [(j, i) for i, j in up]
        last = lax.slice_in_dim(shard, length - width, length, axis=dim)
        initial = lax.slice_in_dim(shard, 0, width, axis=dim)
        before = lax.ppermute(last, axis, up)
        after = lax.ppermute(initial, axis, down)
        shard = jnp.concatenate([before, shard, after], axis=dim)
    return shard


def sinusoid(timesteps, feature_n):
    half_n = feature_n // 2
    freqs = jnp.exp(-math.log(10000.0) * jnp.arange(half_n, dtype=jnp.float32) / half_n)
    angles = timesteps.astype(jnp.float32)[:, None] * freqs[None, :]
    return jnp.concatenate([jnp.cos(angles), jnp.sin(angles)], axis=1)


def group_sums(tensor, groups):
    batch_n, height_n, width_n, channels = tensor.shape
    split = tensor.reshape(batch_n, height_n, width_n, groups, channels // groups)
    return (jnp.sum(split, axis=(1, 2, 4)), jnp.sum(split * split, axis=(1, 2, 4)))


def spread(values, channels):
    return jnp.repeat(values, channels // values.shape[1], axis=1)[:, None, None, :]


def normalize(tensor, first_sum, square_sum, gains, scales, shifts, cell_count):
    channels = tensor.shape[3]
    average = first_sum / cell_count
    inverse = lax.rsqrt(square_sum / cell_count - average * average + EPS)
    normed = (tensor - spread(average, channels)) * spread(inverse, channels) * gains
    return normed * (1.0 + scales[:, None, None, :]) + shifts[:, None, None, :]


def patches(padded, height_n, width_n):
    return jnp.concatenate(
        [
            padded[:, vertical : vertical + height_n, lateral : lateral + width_n, :]
            for vertical in range(3)
            for lateral in range(3)
        ],
        axis=3,
    )


def convolve(padded, matrix):
    batch_n, height_p, width_p, channels = padded.shape
    flat = patches(padded, height_p - 2, width_p - 2).reshape(-1, 9 * channels)
    return jnp.dot(flat, matrix, preferred_element_type=jnp.float32).reshape(
        batch_n, height_p - 2, width_p - 2, matrix.shape[1]
    )


def flip_weight(weight):
    channels = weight.shape[2]
    return jnp.transpose(weight[::-1, ::-1], (0, 1, 3, 2)).reshape(9 * channels, channels)


def silu_slope(pre_act):
    sigmoid_v = jax.nn.sigmoid(pre_act)
    return sigmoid_v * (1.0 + pre_act * (1.0 - sigmoid_v))


def pad_columns(tensor):
    return jnp.pad(tensor, ((0, 0), (0, 0), (1, 1), (0, 0)))


def pick(stacked, index):
    return lax.dynamic_index_in_dim(stacked, index, 0, keepdims=False)


def norm_backward(tensor, first_sum, square_sum, gains, scales, shifts, cell_count, d_pre):

    def mapping(tensor_v, first_v, square_v, gains_v, scales_v, shifts_v):
        return normalize(tensor_v, first_v, square_v, gains_v, scales_v, shifts_v, cell_count)

    _, pull_back = jax.vjp(mapping, tensor, first_sum, square_sum, gains, scales, shifts)
    return pull_back(d_pre)


def per_device(images, steps, out_grad, conv_weight, gn_gain, emb_weight):
    section_count = lax.axis_size("section")
    tick_count = MICRO + section_count - 1
    section_no = lax.axis_index("section")
    local_n = images.shape[0] // MICRO
    row_count = images.shape[1]
    col_count = images.shape[2]
    channels = images.shape[3]
    cell_count = row_count * lax.axis_size("space") * col_count * (channels // G)
    weight = conv_weight[0]
    flat_weight = weight.reshape(9 * channels, channels)
    flipped = flip_weight(weight)
    gains = gn_gain[0]
    all_features = sinusoid(steps, FREQ)
    features = all_features.reshape(MICRO, local_n, FREQ)
    embedded = jnp.dot(
        all_features, emb_weight[0].astype(jnp.float32), precision=lax.Precision.HIGHEST
    ).reshape(MICRO, local_n, 2 * channels)
    batches = images.reshape(MICRO, local_n, row_count, col_count, channels)
    cotangents = out_grad.reshape(MICRO, local_n, row_count, col_count, channels)
    blank = jnp.zeros((local_n, row_count, col_count, channels), jnp.bfloat16)
    carried = blank
    skips = []
    kept_in = []
    kept_first = []
    kept_square = []
    kept_pad = []
    for moment in range(tick_count):
        arrived = blank
        if moment > 0:
            arrived = from_behind(carried, "section", 1)
        inputs = jnp.where(section_no == 0, batches[min(moment, MICRO - 1)], arrived)
        late = moment - (section_count - 1)
        if 0 <= late < MICRO:
            joined = (arrived.astype(jnp.float32) + skips[late].astype(jnp.float32)).astype(
                jnp.bfloat16
            )
            inputs = jnp.where(section_no == section_count - 1, joined, inputs)
        which = jnp.clip(moment - section_no, 0, MICRO - 1)
        chosen = pick(embedded, which)
        tensor = inputs.astype(jnp.float32)
        first_sum, square_sum = group_sums(tensor, G)
        first_sum, square_sum = lax.psum((first_sum, square_sum), "space")
        pre_act = normalize(
            tensor,
            first_sum,
            square_sum,
            gains,
            chosen[:, :channels],
            chosen[:, channels:],
            cell_count,
        )
        activation = jax.nn.silu(pre_act).astype(jnp.bfloat16)
        padded = pad_columns(extended(activation, (("space", 1),), 1))
        conv_out = convolve(padded, flat_weight)
        output = (tensor + conv_out).astype(jnp.bfloat16)
        if moment < MICRO:
            skips.append(from_behind(output, "section", section_count - 1))
        kept_in.append(inputs)
        kept_first.append(first_sum)
        kept_square.append(square_sum)
        kept_pad.append(padded)
        carried = output
    stack_in = jnp.stack(kept_in)
    stack_first = jnp.stack(kept_first)
    stack_square = jnp.stack(kept_square)
    stack_pad = jnp.stack(kept_pad)
    weight_grad = jnp.zeros((9 * channels, channels), jnp.float32)
    gain_grad = jnp.zeros((channels,), jnp.float32)
    emb_grad = jnp.zeros((FREQ, 2 * channels), jnp.float32)
    carried = blank
    skip_grads = []
    for moment in range(tick_count):
        arrived = blank
        if moment > 0:
            arrived = from_behind(carried, "section", -1)
        top_grad = cotangents[moment] if moment < MICRO else blank
        upstream = jnp.where(section_no == section_count - 1, top_grad, arrived)
        early = moment - (section_count - 1)
        if 0 <= early < MICRO:
            joined = (arrived.astype(jnp.float32) + skip_grads[early].astype(jnp.float32)).astype(
                jnp.bfloat16
            )
            upstream = jnp.where(section_no == 0, joined, upstream)
        which_raw = moment - (section_count - 1) + section_no
        valid = (which_raw >= 0) & (which_raw < MICRO)
        upstream = jnp.where(valid, upstream, blank)
        which = jnp.clip(which_raw, 0, MICRO - 1)
        forward_at = jnp.clip(which_raw + section_no, 0, tick_count - 1)
        tensor = pick(stack_in, forward_at).astype(jnp.float32)
        first_sum = pick(stack_first, forward_at)
        square_sum = pick(stack_square, forward_at)
        chosen = pick(embedded, which)
        scales = chosen[:, :channels]
        shifts = chosen[:, channels:]
        pre_act = normalize(tensor, first_sum, square_sum, gains, scales, shifts, cell_count)
        padded = pick(stack_pad, forward_at)
        flat_patch = patches(padded, row_count, col_count).reshape(-1, 9 * channels)
        weight_grad = weight_grad + jnp.dot(
            flat_patch.T, upstream.reshape(-1, channels), preferred_element_type=jnp.float32
        )
        up_pad = pad_columns(extended(upstream, (("space", 1),), 1))
        d_act = convolve(up_pad, flipped)
        d_pre = d_act * silu_slope(pre_act)
        d_tensor, d_first, d_square, d_gains, d_scales, d_shifts = norm_backward(
            tensor, first_sum, square_sum, gains, scales, shifts, cell_count, d_pre
        )
        d_first, d_square = lax.psum((d_first, d_square), "space")
        d_tensor = d_tensor + spread(d_first, channels) + 2.0 * tensor * spread(d_square, channels)
        d_input = (upstream.astype(jnp.float32) + d_tensor).astype(jnp.bfloat16)
        gain_grad = gain_grad + d_gains
        emb_grad = emb_grad + jnp.dot(
            pick(features, which).T,
            jnp.concatenate([d_scales, d_shifts], axis=1),
            precision=lax.Precision.HIGHEST,
        )
        if moment < MICRO:
            skip_grads.append(from_behind(d_input, "section", -(section_count - 1)))
        carried = d_input
    grads = (weight_grad.reshape(1, 3, 3, channels, channels), gain_grad[None], emb_grad[None])
    totals = lax.psum((grads[0], grads[1], grads[2]), ("dp", "space"))
    return (totals[0], totals[1], totals[2])


def solution(mesh):
    in_specs = (
        P("dp", "space", None, None),
        P("dp"),
        P("dp", "space", None, None),
        P("section", None, None, None, None),
        P("section", None),
        P("section", None, None),
    )
    out_specs = (P("section", None, None, None, None), P("section", None), P("section", None, None))
    return jax.shard_map(
        per_device, mesh=mesh, in_specs=in_specs, out_specs=out_specs, check_vma=False
    )
```

profile of v0, /device:TPU:32, one launch (start us, length us, event | category | flops | bytes accessed | tf_op | source)
XLA Modules:
  0.0 1326.5 jit_solution(16995887459301476496)
XLA Ops:
  9.3 3.0 collective-permute-start.16
  14.3 7.7 all-reduce.19
  25.5 3.0 collective-permute-start
  34.2 10.0 collective-permute-start.9
  52.3 6.5 all-reduce.18
  60.5 3.0 collective-permute-start.3
  70.5 7.2 all-reduce.17
  83.8 5.1 collective-permute-start.8
  91.6 7.8 all-reduce.16
  101.6 3.0 collective-permute-start.10
  106.8 5.8 collective-permute-start.12
  115.2 7.8 all-reduce.15
  126.5 7.2 all-reduce.14
  135.5 7.2 collective-permute-done.18
  149.7 6.1 all-reduce.13
  157.4 6.3 collective-permute-done.21
  172.4 7.5 all-reduce.12
  181.7 6.2 collective-permute-done.24
  194.1 6.9 all-reduce.11
  207.1 6.6 collective-permute-done.28
  215.0 3.6 collective-permute-start.30
  225.3 279.0 %psum.178 = f32[1,256]{1,0:T(1,128)} all-reduce(f32[1,256]{1,0:T(1,128)S(1)} %bitcast.511), channel_id=1, replica_groups=mesh['dp'=32,'section'=4,'space'=4] {'dp','space'}, use_global_device_ids=true, to_apply=%region_60.61 | all-reduce | flops 256 | bytes 2048 | tf_op jit(solution)/shard_map/psum | solution.py:223
  504.3 811.3 %all-reduce.22.cloned.1.call-done = (f32[1,3,3,256,256]{4,3,2,1,0:T(8,128)}, f32[1,256,512]{2,1,0:T(8,128)}) async-done(((f32[1,3,3,256,256]{4,3,2,1,0:T(8,128)}, f32[1,256,512]{2,1,0:T(8,128)}), (f32[1,3,3,256,256]{4,3,2,1,0:T(8,128)}, f32[1,256,512]{2,1,0:T(8,128)})) %all-reduce.22.cloned.1.call-update) | async-done | bytes 2883600 | tf_op jit(solution)/shard_map/psum | solution.py:223
  1315.6 3.3 copy.140
  (424 shorter events, 89.1 us)
Async XLA Ops:
  7.2 1308.4 %all-reduce.22.cloned.1.call-start = ((), (), s32[]{:S(2)}) async-start(), calls=%async_computation | async-start | bytes 5767168 | tf_op jit(solution)/shard_map/psum | solution.py:223
  8.0 37.5 %collective-permute-start.17 = (bf16[1,1,64,256]{3,2,1,0:T(8,128)(2,1)S(1)}, bf16[1,1,64,256]{3,2,1,0:T(8,128)(2,1)S(1)}, u32[]{:S(2)}, u32[]{:S(2)}) collective-permute-start(bf16[1,1,64,256]{3,2,1,0:T(8,128)(2,1)S(1)} %select_select_fusion.2), channel_id=1, source_target_pairs={{1,0},{2,1},{3,2},{5,4},{6,5},{7,6},{9,8},{10,9},{11,10},{13,12},{... | collective-permute-start | bytes 98312 | tf_op jit(solution)/shard_map/ppermute | solution.py:27
  9.3 36.3 %collective-permute-start.16 = (bf16[1,1,64,256]{3,2,1,0:T(8,128)(2,1)S(1)}, bf16[1,1,64,256]{3,2,1,0:T(8,128)(2,1)S(1)}, u32[]{:S(2)}, u32[]{:S(2)}) collective-permute-start(bf16[1,1,64,256]{3,2,1,0:T(8,128)(2,1)S(1)} %select_select_fusion.2), channel_id=1, source_target_pairs={{0,1},{1,2},{2,3},{4,5},{5,6},{6,7},{8,9},{9,10},{10,11},{12,13},{... | collective-permute-start | bytes 98312 | tf_op jit(solution)/shard_map/ppermute | solution.py:26
  24.2 9.0 collective-permute-start.1
  25.5 7.7 collective-permute-start
  34.2 54.7 %collective-permute-start.9 = (bf16[1,1,64,256]{3,2,1,0:T(8,128)(2,1)S(1)}, bf16[1,1,64,256]{3,2,1,0:T(8,128)(2,1)S(1)}, u32[]{:S(2)}, u32[]{:S(2)}) collective-permute-start(bf16[1,1,64,256]{3,2,1,0:T(8,128)(2,1)S(1)} %fusion.8), channel_id=1, source_target_pairs={{0,12},{1,13},{2,14},{3,15},{16,28},{17,29},{18,30},{19,31},{32,44... | collective-permute-start | bytes 98312 | tf_op jit(solution)/shard_map/ppermute | solution.py:16
  44.3 7.0 collective-permute-start.2
  65.0 48.1 %collective-permute-start.13 = (bf16[1,1,64,256]{3,2,1,0:T(8,128)(2,1)S(1)}, bf16[1,1,64,256]{3,2,1,0:T(8,128)(2,1)S(1)}, u32[]{:S(2)}, u32[]{:S(2)}) collective-permute-start(bf16[1,1,64,256]{3,2,1,0:T(8,128)(2,1)S(1)} %fusion.6), channel_id=1, source_target_pairs={{0,12},{1,13},{2,14},{3,15},{16,28},{17,29},{18,30},{19,31},{32,44... | collective-permute-start | bytes 98312 | tf_op jit(solution)/shard_map/ppermute | solution.py:16
  83.8 6.7 collective-permute-start.8
  106.8 7.3 collective-permute-start.12
  134.1 8.5 collective-permute-start.18
  142.6 6.0 collective-permute-start.20
  143.9 4.7 collective-permute-start.19
  147.0 34.7 %collective-permute-start.25 = (bf16[1,1,64,256]{3,2,1,0:T(8,128)(2,1)S(1)}, bf16[1,1,64,256]{3,2,1,0:T(8,128)(2,1)S(1)}, u32[]{:S(2)}, u32[]{:S(2)}) collective-permute-start(bf16[1,1,64,256]{3,2,1,0:T(8,128)(2,1)S(1)} %fusion.123), channel_id=1, source_target_pairs={{12,0},{13,1},{14,2},{15,3},{28,16},{29,17},{30,18},{31,19},{44,32... | collective-permute-start | bytes 98312 | tf_op jit(solution)/shard_map/ppermute | solution.py:16
  156.1 7.6 collective-permute-start.21
  163.8 7.6 collective-permute-start.23
  165.1 6.3 collective-permute-start.22
  170.0 37.1 %collective-permute-start.29 = (bf16[1,1,64,256]{3,2,1,0:T(8,128)(2,1)S(1)}, bf16[1,1,64,256]{3,2,1,0:T(8,128)(2,1)S(1)}, u32[]{:S(2)}, u32[]{:S(2)}) collective-permute-start(bf16[1,1,64,256]{3,2,1,0:T(8,128)(2,1)S(1)} %fusion.75), channel_id=1, source_target_pairs={{12,0},{13,1},{14,2},{15,3},{28,16},{29,17},{30,18},{31,19},{44,32... | collective-permute-start | bytes 98312 | tf_op jit(solution)/shard_map/ppermute | solution.py:16
  180.3 7.5 collective-permute-start.24
  201.4 17.2 %collective-permute-start.15 = (bf16[1,1,64,256]{3,2,1,0:T(8,128)(2,1)S(1)}, bf16[1,1,64,256]{3,2,1,0:T(8,128)(2,1)S(1)}, u32[]{:S(2)}, u32[]{:S(2)}) collective-permute-start(bf16[1,1,64,256]{3,2,1,0:T(8,128)(2,1)S(1)} %get-tuple-element.118), channel_id=1, source_target_pairs={{1,0},{2,1},{3,2},{5,4},{6,5},{7,6},{9,8},{10,9},{11,10},{13,12},{... | collective-permute-start | bytes 98312 | tf_op jit(solution)/shard_map/ppermute | solution.py:27
  202.7 15.9 %collective-permute-start.14 = (bf16[1,1,64,256]{3,2,1,0:T(8,128)(2,1)S(1)}, bf16[1,1,64,256]{3,2,1,0:T(8,128)(2,1)S(1)}, u32[]{:S(2)}, u32[]{:S(2)}) collective-permute-start(bf16[1,1,64,256]{3,2,1,0:T(8,128)(2,1)S(1)} %get-tuple-element.118), channel_id=1, source_target_pairs={{0,1},{1,2},{2,3},{4,5},{5,6},{6,7},{8,9},{9,10},{10,11},{12,13},{... | collective-permute-start | bytes 98312 | tf_op jit(solution)/shard_map/ppermute | solution.py:26
  205.8 7.9 collective-permute-start.28
  213.7 9.8 collective-permute-start.31
  215.0 8.5 collective-permute-start.30
  (37 other events, 314.8 us)
Sparse Core Ops, SparseCore 0:
  225.4 1090.1 all-reduce.21
where the time goes:
time: 1330 us
  waiting for transfers between devices  845 us (64%)
  blocking collectives  344 us (26%)
  starting transfers between devices  76.6 us (6%)
  local copies, waits for them, and re-layouts  20.9 us (2%)
  between operations  16.3 us (1%)
  other arithmetic  15.7 us (1%)
    psum x1, waiting for transfers between devices, per_device(): totals = lax.psum((grads[0], grads[1], grads[2]), ('dp', 'space'))  811 us
    psum x1, blocking collectives, per_device(): totals = lax.psum((grads[0], grads[1], grads[2]), ('dp', 'space'))  279 us
    psum x5, blocking collectives, per_device(): first_sum, square_sum = lax.psum((first_sum, square_sum), 'space')  36.9 us
    ppermute x12, starting transfers between devices, from_behind(): lax.ppermute(value, axis, [(source, source + steps) for source in range(i...  32.8 us
    ppermute x10, starting transfers between devices, extended(): before = lax.ppermute(last, axis, up)  30.9 us
    ppermute x12, waiting for transfers between devices, from_behind(): lax.ppermute(value, axis, [(source, source + steps) for source in range(i...  30.4 us
    psum x4, blocking collectives, per_device(): d_first, d_square = lax.psum((d_first, d_square), 'space')  27.7 us
  transfers between devices with their start and end apart: 33, of which 12 were waited for; matrix products, arithmetic and copies ran while one was open for 2% of the time, Pallas kernels for 0%

commit v1 on v0

--- a/solution.py
+++ b/solution.py
@@ -220,7 +220,9 @@
             skip_grads.append(from_behind(d_input, "section", -(section_count - 1)))
         carried = d_input
     grads = (weight_grad.reshape(1, 3, 3, channels, channels), gain_grad[None], emb_grad[None])
-    totals = lax.psum((grads[0], grads[1], grads[2]), ("dp", "space"))
+    totals = (grads[0], grads[1], grads[2])
+    for u in ("dp", "space"):
+        totals = jax.lax.psum(totals, axis_name=u)
     return (totals[0], totals[1], totals[2])
 
 

time: 1330 us -> 490 us (0.37)
  the two profiles are of different devices: /device:TPU:32 before, /device:TPU:1 now
where the time goes in v1:
time: 490 us; the launch traced here: 489 us
  waiting for transfers between devices  196 us (40%)
  blocking collectives  136 us (28%)
  starting transfers between devices  94.5 us (19%)
  local copies, waits for them, and re-layouts  20.9 us (4%)
  between operations  16.3 us (3%)
  other arithmetic  15.7 us (3%)
  matrix products  8.35 us (2%)
    psum x2, waiting for transfers between devices, per_device(): totals = jax.lax.psum(totals, axis_name=u)  167 us
    psum x2, blocking collectives, per_device(): totals = jax.lax.psum(totals, axis_name=u)  82.5 us
    ppermute x10, starting transfers between devices, extended(): after = lax.ppermute(initial, axis, down)  34.5 us
    ppermute x10, starting transfers between devices, extended(): before = lax.ppermute(last, axis, up)  31.7 us
    psum x5, blocking collectives, per_device(): first_sum, square_sum = lax.psum((first_sum, square_sum), 'space')  31.5 us
    ppermute x12, starting transfers between devices, from_behind(): lax.ppermute(value, axis, [(source, source + steps) for source in range(i...  28.2 us
    ppermute x12, waiting for transfers between devices, from_behind(): lax.ppermute(value, axis, [(source, source + steps) for source in range(i...  25.4 us
    psum x4, blocking collectives, per_device(): d_first, d_square = lax.psum((d_first, d_square), 'space')  22.4 us
  transfers between devices with their start and end apart: 34, of which 13 were waited for; matrix products, arithmetic and copies ran while one was open for 7% of the time, Pallas kernels for 0%

profile of v1, /device:TPU:1, one launch (start us, length us, event | category | flops | bytes accessed | tf_op | source)
XLA Modules:
  0.0 488.7 jit_solution(9658178572389038666)
XLA Ops:
  8.0 8.8 %collective-permute-start.17 = (bf16[1,1,64,256]{3,2,1,0:T(8,128)(2,1)S(1)}, bf16[1,1,64,256]{3,2,1,0:T(8,128)(2,1)S(1)}, u32[]{:S(2)}, u32[]{:S(2)}) collective-permute-start(bf16[1,1,64,256]{3,2,1,0:T(8,128)(2,1)S(1)} %select_select_fusion.2), channel_id=1, source_target_pairs={{1,0},{2,1},{3,2},{5,4},{6,5},{7,6},{9,8},{10,9},{11,10},{13,12},{... | collective-permute-start | bytes 98312 | tf_op jit(solution)/shard_map/ppermute | solution.py:27
  20.7 5.5 %all-reduce.19 = (f32[1,32]{1,0:T(1,128)S(1)}, f32[1,32]{1,0:T(1,128)S(1)}) all-reduce(f32[1,32]{1,0:T(1,128)S(1)} %bitcast.533, f32[1,32]{1,0:T(1,128)S(1)} %bitcast.532), channel_id=1, replica_groups=mesh['dp'=32,'section'=4,'space'=4] {'space'}, use_global_device_ids=true, to_apply=%region_5.6 | all-reduce | flops 64 | bytes 512 | tf_op jit(solution)/shard_map/psum | solution.py:145
  39.9 6.3 %collective-permute-start.9 = (bf16[1,1,64,256]{3,2,1,0:T(8,128)(2,1)S(1)}, bf16[1,1,64,256]{3,2,1,0:T(8,128)(2,1)S(1)}, u32[]{:S(2)}, u32[]{:S(2)}) collective-permute-start(bf16[1,1,64,256]{3,2,1,0:T(8,128)(2,1)S(1)} %fusion.8), channel_id=1, source_target_pairs={{0,12},{1,13},{2,14},{3,15},{16,28},{17,29},{18,30},{19,31},{32,44... | collective-permute-start | bytes 98312 | tf_op jit(solution)/shard_map/ppermute | solution.py:16
  54.2 5.1 %all-reduce.18 = (f32[1,32]{1,0:T(1,128)S(1)}, f32[1,32]{1,0:T(1,128)S(1)}) all-reduce(f32[1,32]{1,0:T(1,128)S(1)} %bitcast.534, f32[1,32]{1,0:T(1,128)S(1)} %bitcast.528), channel_id=1, replica_groups=mesh['dp'=32,'section'=4,'space'=4] {'space'}, use_global_device_ids=true, to_apply=%region_11.12 | all-reduce | flops 64 | bytes 512 | tf_op jit(solution)/shard_map/psum | solution.py:145
  72.0 7.0 %all-reduce.17 = (f32[1,32]{1,0:T(1,128)S(1)}, f32[1,32]{1,0:T(1,128)S(1)}) all-reduce(f32[1,32]{1,0:T(1,128)S(1)} %bitcast.535, f32[1,32]{1,0:T(1,128)S(1)} %bitcast.529), channel_id=1, replica_groups=mesh['dp'=32,'section'=4,'space'=4] {'space'}, use_global_device_ids=true, to_apply=%region_17.18 | all-reduce | flops 64 | bytes 512 | tf_op jit(solution)/shard_map/psum | solution.py:145
  81.5 3.7 collective-permute-start.6
  86.8 4.8 collective-permute-start.8
  93.7 7.0 %all-reduce.16 = (f32[1,32]{1,0:T(1,128)S(1)}, f32[1,32]{1,0:T(1,128)S(1)}) all-reduce(f32[1,32]{1,0:T(1,128)S(1)} %bitcast.536, f32[1,32]{1,0:T(1,128)S(1)} %bitcast.530), channel_id=1, replica_groups=mesh['dp'=32,'section'=4,'space'=4] {'space'}, use_global_device_ids=true, to_apply=%region_23.24 | all-reduce | flops 64 | bytes 512 | tf_op jit(solution)/shard_map/psum | solution.py:145
  109.8 5.5 %collective-permute-start.12 = (bf16[1,1,64,256]{3,2,1,0:T(8,128)(2,1)S(1)}, bf16[1,1,64,256]{3,2,1,0:T(8,128)(2,1)S(1)}, u32[]{:S(2)}, u32[]{:S(2)}) collective-permute-start(bf16[1,1,64,256]{3,2,1,0:T(8,128)(2,1)S(1)} %fusion.4), channel_id=1, source_target_pairs={{0,4},{4,8},{8,12},{1,5},{5,9},{9,13},{2,6},{6,10},{10,14},{3,7},{... | collective-permute-start | bytes 98312 | tf_op jit(solution)/shard_map/ppermute | solution.py:16
  117.3 7.0 %all-reduce.15 = (f32[1,32]{1,0:T(1,128)S(1)}, f32[1,32]{1,0:T(1,128)S(1)}) all-reduce(f32[1,32]{1,0:T(1,128)S(1)} %bitcast.537, f32[1,32]{1,0:T(1,128)S(1)} %bitcast.531), channel_id=1, replica_groups=mesh['dp'=32,'section'=4,'space'=4] {'space'}, use_global_device_ids=true, to_apply=%region_29.30 | all-reduce | flops 64 | bytes 512 | tf_op jit(solution)/shard_map/psum | solution.py:145
  127.8 5.8 %all-reduce.14 = (f32[1,32]{1,0:T(1,128)S(1)}, f32[32]{0:T(128)S(1)}) all-reduce(f32[1,32]{1,0:T(1,128)S(1)} %broadcast_multiply_fusion.3, f32[32]{0:T(128)S(1)} %get-tuple-element.70), channel_id=1, replica_groups=mesh['dp'=32,'section'=4,'space'=4] {'space'}, use_global_device_ids=true, to_apply=%region_35.36 | all-reduce | flops 64 | bytes 512 | tf_op jit(solution)/shard_map/psum | solution.py:210
  135.3 5.9 %collective-permute-done.18 = bf16[1,1,64,256]{3,2,1,0:T(8,128)(2,1)S(1)} collective-permute-done((bf16[1,1,64,256]{3,2,1,0:T(8,128)(2,1)S(1)}, bf16[1,1,64,256]{3,2,1,0:T(8,128)(2,1)S(1)}, u32[]{:S(2)}, u32[]{:S(2)}) %collective-permute-start.18) | collective-permute-done | bytes 32800 | tf_op jit(solution)/shard_map/ppermute | solution.py:16
  141.3 4.8 collective-permute-start.20
  150.8 5.4 %all-reduce.13 = (f32[1,32]{1,0:T(1,128)S(1)}, f32[32]{0:T(128)S(1)}) all-reduce(f32[1,32]{1,0:T(1,128)S(1)} %broadcast_multiply_fusion.2, f32[32]{0:T(128)S(1)} %get-tuple-element.66), channel_id=1, replica_groups=mesh['dp'=32,'section'=4,'space'=4] {'space'}, use_global_device_ids=true, to_apply=%region_41.42 | all-reduce | flops 64 | bytes 512 | tf_op jit(solution)/shard_map/psum | solution.py:210
  157.9 6.2 %collective-permute-done.21 = bf16[1,1,64,256]{3,2,1,0:T(8,128)(2,1)S(1)} collective-permute-done((bf16[1,1,64,256]{3,2,1,0:T(8,128)(2,1)S(1)}, bf16[1,1,64,256]{3,2,1,0:T(8,128)(2,1)S(1)}, u32[]{:S(2)}, u32[]{:S(2)}) %collective-permute-start.21) | collective-permute-done | bytes 32800 | tf_op jit(solution)/shard_map/ppermute | solution.py:16
  175.2 5.1 %all-reduce.12 = (f32[1,32]{1,0:T(1,128)S(1)}, f32[32]{0:T(128)S(1)}) all-reduce(f32[1,32]{1,0:T(1,128)S(1)} %broadcast_multiply_fusion.1, f32[32]{0:T(128)S(1)} %get-tuple-element.62), channel_id=1, replica_groups=mesh['dp'=32,'section'=4,'space'=4] {'space'}, use_global_device_ids=true, to_apply=%region_47.48 | all-reduce | flops 64 | bytes 512 | tf_op jit(solution)/shard_map/psum | solution.py:210
  182.0 5.1 %collective-permute-done.24 = bf16[1,1,64,256]{3,2,1,0:T(8,128)(2,1)S(1)} collective-permute-done((bf16[1,1,64,256]{3,2,1,0:T(8,128)(2,1)S(1)}, bf16[1,1,64,256]{3,2,1,0:T(8,128)(2,1)S(1)}, u32[]{:S(2)}, u32[]{:S(2)}) %collective-permute-start.24) | collective-permute-done | bytes 32800 | tf_op jit(solution)/shard_map/ppermute | solution.py:16
  187.1 4.2 collective-permute-start.27
  196.2 6.1 %all-reduce.11 = (f32[1,32]{1,0:T(1,128)S(1)}, f32[32]{0:T(128)S(1)}) all-reduce(f32[1,32]{1,0:T(1,128)S(1)} %broadcast_multiply_fusion, f32[32]{0:T(128)S(1)} %get-tuple-element.58), channel_id=1, replica_groups=mesh['dp'=32,'section'=4,'space'=4] {'space'}, use_global_device_ids=true, to_apply=%region_53.54 | all-reduce | flops 64 | bytes 512 | tf_op jit(solution)/shard_map/psum | solution.py:210
  209.9 5.7 %collective-permute-done.28 = bf16[1,1,64,256]{3,2,1,0:T(8,128)(2,1)S(1)} collective-permute-done((bf16[1,1,64,256]{3,2,1,0:T(8,128)(2,1)S(1)}, bf16[1,1,64,256]{3,2,1,0:T(8,128)(2,1)S(1)}, u32[]{:S(2)}, u32[]{:S(2)}) %collective-permute-start.28) | collective-permute-done | bytes 32800 | tf_op jit(solution)/shard_map/ppermute | solution.py:16
  217.5 3.8 collective-permute-start.30
  228.1 163.4 %all-reduce.24.cloned.1.call-done = (f32[1,3,3,256,256]{4,3,2,1,0:T(8,128)}, f32[1,256,512]{2,1,0:T(8,128)}) async-done(((f32[1,3,3,256,256]{4,3,2,1,0:T(8,128)}, f32[1,256,512]{2,1,0:T(8,128)}), (f32[1,3,3,256,256]{4,3,2,1,0:T(8,128)}, f32[1,256,512]{2,1,0:T(8,128)})) %all-reduce.24.cloned.1.call-update) | async-done | bytes 2883600 | tf_op jit(solution)/shard_map/psum | solution.py:225
  391.5 58.6 %psum.200 = f32[1,256]{1,0:T(1,128)S(1)} all-reduce(f32[1,256]{1,0:T(1,128)S(1)} %bitcast.511), channel_id=1, replica_groups=mesh['dp'=32,'section'=4,'space'=4] {'dp'}, use_global_device_ids=true, to_apply=%region_61.62 | all-reduce | flops 256 | bytes 2048 | tf_op jit(solution)/shard_map/psum | solution.py:225
  450.2 23.8 %psum.201 = f32[1,256]{1,0:T(1,128)} all-reduce(f32[1,256]{1,0:T(1,128)S(1)} %psum.200), channel_id=1, replica_groups=mesh['dp'=32,'section'=4,'space'=4] {'space'}, use_global_device_ids=true, to_apply=%region_62.63 | all-reduce | flops 256 | bytes 2048 | tf_op jit(solution)/shard_map/psum | solution.py:225
  (428 shorter events, 107.8 us)
Async XLA Ops:
  7.2 384.3 %all-reduce.24.cloned.1.call-start = ((), (), s32[]{:S(2)}) async-start(), calls=%async_computation | async-start | bytes 5767168 | tf_op jit(solution)/shard_map/psum | solution.py:225
  8.0 39.4 %collective-permute-start.17 = (bf16[1,1,64,256]{3,2,1,0:T(8,128)(2,1)S(1)}, bf16[1,1,64,256]{3,2,1,0:T(8,128)(2,1)S(1)}, u32[]{:S(2)}, u32[]{:S(2)}) collective-permute-start(bf16[1,1,64,256]{3,2,1,0:T(8,128)(2,1)S(1)} %select_select_fusion.2), channel_id=1, source_target_pairs={{1,0},{2,1},{3,2},{5,4},{6,5},{7,6},{9,8},{10,9},{11,10},{13,12},{... | collective-permute-start | bytes 98312 | tf_op jit(solution)/shard_map/ppermute | solution.py:27
  16.8 30.6 %collective-permute-start.16 = (bf16[1,1,64,256]{3,2,1,0:T(8,128)(2,1)S(1)}, bf16[1,1,64,256]{3,2,1,0:T(8,128)(2,1)S(1)}, u32[]{:S(2)}, u32[]{:S(2)}) collective-permute-start(bf16[1,1,64,256]{3,2,1,0:T(8,128)(2,1)S(1)} %select_select_fusion.2), channel_id=1, source_target_pairs={{0,1},{1,2},{2,3},{4,5},{5,6},{6,7},{8,9},{9,10},{10,11},{12,13},{... | collective-permute-start | bytes 98312 | tf_op jit(solution)/shard_map/ppermute | solution.py:26
  28.4 10.5 %collective-permute-start.1 = (bf16[1,1,64,256]{3,2,1,0:T(8,128)(2,1)S(1)}, bf16[1,1,64,256]{3,2,1,0:T(8,128)(2,1)S(1)}, u32[]{:S(2)}, u32[]{:S(2)}) collective-permute-start(bf16[1,1,64,256]{3,2,1,0:T(8,128)(2,1)S(1)} %multiply_convert_fusion.4), channel_id=1, source_target_pairs={{1,0},{2,1},{3,2},{5,4},{6,5},{7,6},{9,8},{10,9},{11,10},{13,12},{... | collective-permute-start | bytes 98312 | tf_op jit(solution)/shard_map/ppermute | solution.py:27
  31.0 7.9 %collective-permute-start = (bf16[1,1,64,256]{3,2,1,0:T(8,128)(2,1)S(1)}, bf16[1,1,64,256]{3,2,1,0:T(8,128)(2,1)S(1)}, u32[]{:S(2)}, u32[]{:S(2)}) collective-permute-start(bf16[1,1,64,256]{3,2,1,0:T(8,128)(2,1)S(1)} %multiply_convert_fusion.4), channel_id=1, source_target_pairs={{0,1},{1,2},{2,3},{4,5},{5,6},{6,7},{8,9},{9,10},{10,11},{12,13},{... | collective-permute-start | bytes 98312 | tf_op jit(solution)/shard_map/ppermute | solution.py:26
  39.9 51.8 %collective-permute-start.9 = (bf16[1,1,64,256]{3,2,1,0:T(8,128)(2,1)S(1)}, bf16[1,1,64,256]{3,2,1,0:T(8,128)(2,1)S(1)}, u32[]{:S(2)}, u32[]{:S(2)}) collective-permute-start(bf16[1,1,64,256]{3,2,1,0:T(8,128)(2,1)S(1)} %fusion.8), channel_id=1, source_target_pairs={{0,12},{1,13},{2,14},{3,15},{16,28},{17,29},{18,30},{19,31},{32,44... | collective-permute-start | bytes 98312 | tf_op jit(solution)/shard_map/ppermute | solution.py:16
  46.1 7.0 %collective-permute-start.2 = (bf16[1,1,64,256]{3,2,1,0:T(8,128)(2,1)S(1)}, bf16[1,1,64,256]{3,2,1,0:T(8,128)(2,1)S(1)}, u32[]{:S(2)}, u32[]{:S(2)}) collective-permute-start(bf16[1,1,64,256]{3,2,1,0:T(8,128)(2,1)S(1)} %fusion.8), channel_id=1, source_target_pairs={{0,4},{4,8},{8,12},{1,5},{5,9},{9,13},{2,6},{6,10},{10,14},{3,7},{... | collective-permute-start | bytes 98312 | tf_op jit(solution)/shard_map/ppermute | solution.py:16
  67.4 48.4 %collective-permute-start.13 = (bf16[1,1,64,256]{3,2,1,0:T(8,128)(2,1)S(1)}, bf16[1,1,64,256]{3,2,1,0:T(8,128)(2,1)S(1)}, u32[]{:S(2)}, u32[]{:S(2)}) collective-permute-start(bf16[1,1,64,256]{3,2,1,0:T(8,128)(2,1)S(1)} %fusion.6), channel_id=1, source_target_pairs={{0,12},{1,13},{2,14},{3,15},{16,28},{17,29},{18,30},{19,31},{32,44... | collective-permute-start | bytes 98312 | tf_op jit(solution)/shard_map/ppermute | solution.py:16
  109.8 6.5 %collective-permute-start.12 = (bf16[1,1,64,256]{3,2,1,0:T(8,128)(2,1)S(1)}, bf16[1,1,64,256]{3,2,1,0:T(8,128)(2,1)S(1)}, u32[]{:S(2)}, u32[]{:S(2)}) collective-permute-start(bf16[1,1,64,256]{3,2,1,0:T(8,128)(2,1)S(1)} %fusion.4), channel_id=1, source_target_pairs={{0,4},{4,8},{8,12},{1,5},{5,9},{9,13},{2,6},{6,10},{10,14},{3,7},{... | collective-permute-start | bytes 98312 | tf_op jit(solution)/shard_map/ppermute | solution.py:16
  134.0 7.3 %collective-permute-start.18 = (bf16[1,1,64,256]{3,2,1,0:T(8,128)(2,1)S(1)}, bf16[1,1,64,256]{3,2,1,0:T(8,128)(2,1)S(1)}, u32[]{:S(2)}, u32[]{:S(2)}) collective-permute-start(bf16[1,1,64,256]{3,2,1,0:T(8,128)(2,1)S(1)} %fusion.123), channel_id=1, source_target_pairs={{4,0},{8,4},{12,8},{5,1},{9,5},{13,9},{6,2},{10,6},{14,10},{7,3},{... | collective-permute-start | bytes 98312 | tf_op jit(solution)/shard_map/ppermute | solution.py:16
  141.3 8.4 %collective-permute-start.20 = (bf16[1,1,64,256]{3,2,1,0:T(8,128)(2,1)S(1)}, bf16[1,1,64,256]{3,2,1,0:T(8,128)(2,1)S(1)}, u32[]{:S(2)}, u32[]{:S(2)}) collective-permute-start(bf16[1,1,64,256]{3,2,1,0:T(8,128)(2,1)S(1)} %select_select_fusion.1), channel_id=1, source_target_pairs={{1,0},{2,1},{3,2},{5,4},{6,5},{7,6},{9,8},{10,9},{11,10},{13,12},{... | collective-permute-start | bytes 98312 | tf_op jit(solution)/shard_map/ppermute | solution.py:27
  148.1 33.9 %collective-permute-start.25 = (bf16[1,1,64,256]{3,2,1,0:T(8,128)(2,1)S(1)}, bf16[1,1,64,256]{3,2,1,0:T(8,128)(2,1)S(1)}, u32[]{:S(2)}, u32[]{:S(2)}) collective-permute-start(bf16[1,1,64,256]{3,2,1,0:T(8,128)(2,1)S(1)} %fusion.123), channel_id=1, source_target_pairs={{12,0},{13,1},{14,2},{15,3},{28,16},{29,17},{30,18},{31,19},{44,32... | collective-permute-start | bytes 98312 | tf_op jit(solution)/shard_map/ppermute | solution.py:16
  156.6 7.6 %collective-permute-start.21 = (bf16[1,1,64,256]{3,2,1,0:T(8,128)(2,1)S(1)}, bf16[1,1,64,256]{3,2,1,0:T(8,128)(2,1)S(1)}, u32[]{:S(2)}, u32[]{:S(2)}) collective-permute-start(bf16[1,1,64,256]{3,2,1,0:T(8,128)(2,1)S(1)} %fusion.75), channel_id=1, source_target_pairs={{4,0},{8,4},{12,8},{5,1},{9,5},{13,9},{6,2},{10,6},{14,10},{7,3},{... | collective-permute-start | bytes 98312 | tf_op jit(solution)/shard_map/ppermute | solution.py:16
  164.2 9.9 %collective-permute-start.23 = (bf16[1,1,64,256]{3,2,1,0:T(8,128)(2,1)S(1)}, bf16[1,1,64,256]{3,2,1,0:T(8,128)(2,1)S(1)}, u32[]{:S(2)}, u32[]{:S(2)}) collective-permute-start(bf16[1,1,64,256]{3,2,1,0:T(8,128)(2,1)S(1)} %select_select_fusion), channel_id=1, source_target_pairs={{1,0},{2,1},{3,2},{5,4},{6,5},{7,6},{9,8},{10,9},{11,10},{13,12},{... | collective-permute-start | bytes 98312 | tf_op jit(solution)/shard_map/ppermute | solution.py:27
  167.2 6.9 %collective-permute-start.22 = (bf16[1,1,64,256]{3,2,1,0:T(8,128)(2,1)S(1)}, bf16[1,1,64,256]{3,2,1,0:T(8,128)(2,1)S(1)}, u32[]{:S(2)}, u32[]{:S(2)}) collective-permute-start(bf16[1,1,64,256]{3,2,1,0:T(8,128)(2,1)S(1)} %select_select_fusion), channel_id=1, source_target_pairs={{0,1},{1,2},{2,3},{4,5},{5,6},{6,7},{8,9},{9,10},{10,11},{12,13},{... | collective-permute-start | bytes 98312 | tf_op jit(solution)/shard_map/ppermute | solution.py:26
  172.8 37.1 %collective-permute-start.29 = (bf16[1,1,64,256]{3,2,1,0:T(8,128)(2,1)S(1)}, bf16[1,1,64,256]{3,2,1,0:T(8,128)(2,1)S(1)}, u32[]{:S(2)}, u32[]{:S(2)}) collective-permute-start(bf16[1,1,64,256]{3,2,1,0:T(8,128)(2,1)S(1)} %fusion.75), channel_id=1, source_target_pairs={{12,0},{13,1},{14,2},{15,3},{28,16},{29,17},{30,18},{31,19},{44,32... | collective-permute-start | bytes 98312 | tf_op jit(solution)/shard_map/ppermute | solution.py:16
  180.7 6.4 %collective-permute-start.24 = (bf16[1,1,64,256]{3,2,1,0:T(8,128)(2,1)S(1)}, bf16[1,1,64,256]{3,2,1,0:T(8,128)(2,1)S(1)}, u32[]{:S(2)}, u32[]{:S(2)}) collective-permute-start(bf16[1,1,64,256]{3,2,1,0:T(8,128)(2,1)S(1)} %fusion.79), channel_id=1, source_target_pairs={{4,0},{8,4},{12,8},{5,1},{9,5},{13,9},{6,2},{10,6},{14,10},{7,3},{... | collective-permute-start | bytes 98312 | tf_op jit(solution)/shard_map/ppermute | solution.py:16
  187.1 7.0 %collective-permute-start.27 = (bf16[1,1,64,256]{3,2,1,0:T(8,128)(2,1)S(1)}, bf16[1,1,64,256]{3,2,1,0:T(8,128)(2,1)S(1)}, u32[]{:S(2)}, u32[]{:S(2)}) collective-permute-start(bf16[1,1,64,256]{3,2,1,0:T(8,128)(2,1)S(1)} %fusion.120), channel_id=1, source_target_pairs={{1,0},{2,1},{3,2},{5,4},{6,5},{7,6},{9,8},{10,9},{11,10},{13,12},{... | collective-permute-start | bytes 98312 | tf_op jit(solution)/shard_map/ppermute | solution.py:27
  202.7 18.7 %collective-permute-start.15 = (bf16[1,1,64,256]{3,2,1,0:T(8,128)(2,1)S(1)}, bf16[1,1,64,256]{3,2,1,0:T(8,128)(2,1)S(1)}, u32[]{:S(2)}, u32[]{:S(2)}) collective-permute-start(bf16[1,1,64,256]{3,2,1,0:T(8,128)(2,1)S(1)} %get-tuple-element.120), channel_id=1, source_target_pairs={{1,0},{2,1},{3,2},{5,4},{6,5},{7,6},{9,8},{10,9},{11,10},{13,12},{... | collective-permute-start | bytes 98312 | tf_op jit(solution)/shard_map/ppermute | solution.py:27
  204.9 16.5 %collective-permute-start.14 = (bf16[1,1,64,256]{3,2,1,0:T(8,128)(2,1)S(1)}, bf16[1,1,64,256]{3,2,1,0:T(8,128)(2,1)S(1)}, u32[]{:S(2)}, u32[]{:S(2)}) collective-permute-start(bf16[1,1,64,256]{3,2,1,0:T(8,128)(2,1)S(1)} %get-tuple-element.120), channel_id=1, source_target_pairs={{0,1},{1,2},{2,3},{4,5},{5,6},{6,7},{8,9},{9,10},{10,11},{12,13},{... | collective-permute-start | bytes 98312 | tf_op jit(solution)/shard_map/ppermute | solution.py:26
  208.5 7.0 %collective-permute-start.28 = (bf16[1,1,64,256]{3,2,1,0:T(8,128)(2,1)S(1)}, bf16[1,1,64,256]{3,2,1,0:T(8,128)(2,1)S(1)}, u32[]{:S(2)}, u32[]{:S(2)}) collective-permute-start(bf16[1,1,64,256]{3,2,1,0:T(8,128)(2,1)S(1)} %get-tuple-element.119), channel_id=1, source_target_pairs={{4,0},{8,4},{12,8},{5,1},{9,5},{13,9},{6,2},{10,6},{14,10},{7,3},{... | collective-permute-start | bytes 98312 | tf_op jit(solution)/shard_map/ppermute | solution.py:16
  215.6 10.7 %collective-permute-start.31 = (bf16[1,1,64,256]{3,2,1,0:T(8,128)(2,1)S(1)}, bf16[1,1,64,256]{3,2,1,0:T(8,128)(2,1)S(1)}, u32[]{:S(2)}, u32[]{:S(2)}) collective-permute-start(bf16[1,1,64,256]{3,2,1,0:T(8,128)(2,1)S(1)} %fusion.122), channel_id=1, source_target_pairs={{1,0},{2,1},{3,2},{5,4},{6,5},{7,6},{9,8},{10,9},{11,10},{13,12},{... | collective-permute-start | bytes 98312 | tf_op jit(solution)/shard_map/ppermute | solution.py:27
  217.5 8.8 %collective-permute-start.30 = (bf16[1,1,64,256]{3,2,1,0:T(8,128)(2,1)S(1)}, bf16[1,1,64,256]{3,2,1,0:T(8,128)(2,1)S(1)}, u32[]{:S(2)}, u32[]{:S(2)}) collective-permute-start(bf16[1,1,64,256]{3,2,1,0:T(8,128)(2,1)S(1)} %fusion.122), channel_id=1, source_target_pairs={{0,1},{1,2},{2,3},{4,5},{5,6},{6,7},{8,9},{9,10},{10,11},{12,13},{... | collective-permute-start | bytes 98312 | tf_op jit(solution)/shard_map/ppermute | solution.py:26
  228.0 249.7 %all-reduce.26.cloned.1.call-start = ((), (), s32[]{:S(2)}) async-start(), calls=%async_computation.1 | async-start | bytes 5767168 | tf_op jit(solution)/shard_map/psum | solution.py:225
  (38 other events, 320.9 us)
Sparse Core Ops, SparseCore 0:
  228.2 163.2 all-reduce.23
  394.8 82.8 all-reduce.25
